TPU v7x, 256 devices: a whole 4x4x8 slice. The times are simulated.
256 devices in a mesh: space: 64 (over x_hi, y, z), dp: 4 (over x_lo, core).
Axes of the slice: x: 4 (x_hi: 2, x_lo: 2; x = x_hi * 2 + x_lo), y: 4, z: 8, core: 2. Of those that a mesh axis runs over, the one named last changes fastest.
Arguments:
- input_states: bfloat16 [4, 64, 200, 1024], P('dp', 'space'), may hold values from -6 to 6
- loss_sensitivity: bfloat16 [4, 64, 200, 1024], P('dp', 'space'), may hold values from -6 to 6
- ocean: int32 [64, 1024], P('space'), may hold values 0 or 1
- neighbours: int32 [64, 8], P('space'), may hold values from -1 to 63, as said below
- fold_flag: int32 [64], P('space'), may hold values from 0 to 1, as said below
- w_first: bfloat16 [9, 200, 200], replicated, may hold values from -0.125 to 0.125
- w_second: bfloat16 [9, 200, 200], replicated, may hold values from -0.125 to 0.125
Outputs:
- prediction: bfloat16 [4, 64, 200, 1024], P('dp', 'space')
- earlier_kernel_slope: float32 [9, 200, 200], replicated
- latter_kernel_slope: float32 [9, 200, 200], replicated
Inputs may be any that keep to these rules, and one draw needn't show every extreme that they name: Tiles sit on a grid of 6 x 16 tile positions, some of them land; the ocean tiles carry numbers 0 to 63 in no particular order of positions; longitude wraps; the top row's northern neighbour is the mirrored tile of the same row (fold_flag 1) and its diagonal northern neighbours are -1. The relation is symmetric: if u is t's neighbour in one direction, t is u's in the opposite one (north for north across the fold). `fold_flag`: 1 exactly for tiles of the top tile row.
All inputs are finite; a program needn't handle non-finite values. No bound on the sum of `ocean` on one device may be relied on, other than what follows from the above.
Results may differ from a plain program's by a relative error of at most 0.005.
Values may be sent and summed in bfloat16 or wider, within the bound.
No kernel may reach another device: no remote copies, remote signals or barrier semaphores. Data moves between devices by JAX's collectives and lax.ppermute only.
A program may use at most 64 MiB of HBM per device.

v0:
```python
import jax
import jax.numpy as jnp
from jax import lax
from jax.sharding import PartitionSpec as P

SIDE = 32
SQRT_TWO_PI = 0.7978845608028654
CUBIC = 0.044715


def gelu_pair(a):
    inner = SQRT_TWO_PI * (a + CUBIC * a * a * a)
    tangent = jnp.tanh(inner)
    value = 0.5 * a * (1.0 + tangent)
    slope = 0.5 * (1.0 + tangent) + 0.5 * a * (1.0 - tangent * tangent) * SQRT_TWO_PI * (
        1.0 + 3.0 * CUBIC * a * a
    )
    return (value, slope)


def edge_strips(field):
    patch_extent = field.shape[2]
    return jnp.concatenate(
        [
            field[:, :, 0, :],
            field[:, :, patch_extent - 1, :],
            field[:, :, :, 0],
            field[:, :, :, patch_extent - 1],
        ],
        axis=2,
    )


def strip_parts(piece, neighbours, fold_flag):
    amount = piece.shape[0]
    patch_extent = piece.shape[2] // 4

    def pick(k):
        index = neighbours[:, k]
        valid = ((index >= 0) & (index < amount)).astype(piece.dtype)
        return jnp.take(piece, jnp.clip(index, 0, amount - 1), axis=0) * valid[:, None, None]

    from_north = pick(0)
    north = jnp.where(
        (fold_flag == 1)[:, None, None],
        from_north[:, :, patch_extent : 2 * patch_extent][:, :, ::-1],
        from_north[:, :, 0:patch_extent],
    )
    south = pick(1)[:, :, patch_extent : 2 * patch_extent]
    east = pick(2)[:, :, 2 * patch_extent : 3 * patch_extent]
    west = pick(3)[:, :, 3 * patch_extent : 4 * patch_extent]
    corners = jnp.stack(
        [
            pick(4)[:, :, 0],
            pick(5)[:, :, patch_extent - 1],
            pick(6)[:, :, patch_extent],
            pick(7)[:, :, 2 * patch_extent - 1],
        ],
        axis=-1,
    )
    return (north, south, east, west, corners)


def collect_rims(strips, neighbours, fold_flag):
    found = strip_parts(lax.all_gather(strips, "space", axis=0, tiled=True), neighbours, fold_flag)
    return tuple((b for b in found))


def padded_tiles(field, parts):
    north, south, east, west, corners = parts
    middle = jnp.concatenate([west[..., None], field, east[..., None]], axis=3)
    bottom = jnp.concatenate([corners[:, :, 3:4], south, corners[:, :, 2:3]], axis=2)[:, :, None, :]
    top = jnp.concatenate([corners[:, :, 1:2], north, corners[:, :, 0:1]], axis=2)[:, :, None, :]
    return jnp.concatenate([bottom, middle, top], axis=2)


def window(padded, shift_r, shift_c):
    patch_extent = padded.shape[2] - 2
    part = padded[
        :, :, 1 + shift_r : 1 + shift_r + patch_extent, 1 + shift_c : 1 + shift_c + patch_extent
    ]
    return part.reshape(padded.shape[0], padded.shape[1], patch_extent * patch_extent)


def conv_forward(padded, weights):
    total = None
    for k in range(9):
        term = jnp.einsum(
            "oi,tic->toc",
            weights[k],
            window(padded, k // 3 - 1, k % 3 - 1),
            preferred_element_type=jnp.float32,
        )
        total = term if total is None else total + term
    return total


def conv_adjoint(padded, weights):
    total = None
    for k in range(9):
        term = jnp.einsum(
            "oi,toc->tic",
            weights[k],
            window(padded, 1 - k // 3, 1 - k % 3),
            preferred_element_type=jnp.float32,
        )
        total = term if total is None else total + term
    return total


def weight_grad(grads, padded):
    return jnp.stack(
        [
            jnp.einsum(
                "toc,tic->oi",
                grads,
                window(padded, k // 3 - 1, k % 3 - 1),
                preferred_element_type=jnp.float32,
            )
            for k in range(9)
        ],
        axis=0,
    )


def body(input_states, loss_sensitivity, ocean, neighbours, fold_flag, w_first, w_second):
    tiles = input_states[0]
    patch_total, feature_depth, cells = tiles.shape
    patch_extent = SIDE
    inputs = tiles.reshape(patch_total, feature_depth, patch_extent, patch_extent)
    water_indicator = ocean.astype(jnp.float32)[:, None, :]
    masked_grad = (loss_sensitivity[0].astype(jnp.float32) * water_indicator).astype(jnp.bfloat16)
    grad_tiles = masked_grad.reshape(patch_total, feature_depth, patch_extent, patch_extent)
    field_parts = collect_rims(edge_strips(inputs), neighbours, fold_flag)
    in_padded = padded_tiles(inputs, field_parts)
    pre_first = conv_forward(in_padded, w_first)
    value, slope = gelu_pair(pre_first)
    hidden = (value * water_indicator).astype(jnp.bfloat16)
    hidden_tiles = hidden.reshape(patch_total, feature_depth, patch_extent, patch_extent)
    hidden_parts = collect_rims(edge_strips(hidden_tiles), neighbours, fold_flag)
    hidden_padded = padded_tiles(hidden_tiles, hidden_parts)
    latter_linear_response = conv_forward(hidden_padded, w_second)
    prediction = (latter_linear_response * water_indicator).astype(jnp.bfloat16)[None]
    grad_parts = collect_rims(edge_strips(grad_tiles), neighbours, fold_flag)
    grad_padded = padded_tiles(grad_tiles, grad_parts)
    latter_kernel_slope = weight_grad(masked_grad, hidden_padded)
    back = conv_adjoint(grad_padded, w_second).reshape(
        patch_total, feature_depth, patch_extent, patch_extent
    )
    top_row = grad_padded[:, :, patch_extent + 1, :]
    correction = jnp.zeros((patch_total, feature_depth, patch_extent), jnp.float32)
    for shift_c in (-1, 0, 1):
        segment = top_row[:, :, 1 - shift_c : 1 - shift_c + patch_extent]
        correction = correction + jnp.einsum(
            "oi,toc->tic", w_second[7 - shift_c], segment, preferred_element_type=jnp.float32
        )
        correction = correction - jnp.einsum(
            "oi,toc->tic", w_second[1 + shift_c], segment, preferred_element_type=jnp.float32
        )
    flipped = (fold_flag == 1).astype(jnp.float32)[:, None, None]
    back = back.at[:, :, patch_extent - 1, :].add(correction * flipped)
    pre_grad = (back.reshape(patch_total, feature_depth, cells) * water_indicator * slope).astype(
        jnp.bfloat16
    )
    earlier_kernel_slope = weight_grad(pre_grad, in_padded)
    earlier_kernel_slope, latter_kernel_slope = lax.psum(
        (earlier_kernel_slope, latter_kernel_slope), ("space", "dp")
    )
    return (prediction, earlier_kernel_slope, latter_kernel_slope)


def solution(mesh):
    placed = (
        P("dp", "space", None, None),
        P("dp", "space", None, None),
        P("space", None),
        P("space", None),
        P("space"),
        P(),
        P(),
    )
    return jax.shard_map(
        body,
        mesh=mesh,
        in_specs=placed,
        out_specs=(P("dp", "space", None, None), P(), P()),
        check_vma=False,
    )
```

profile of v0, /device:TPU:2, one launch (start us, length us, event | category | flops | bytes accessed | tf_op | source)
XLA Modules:
  0.0 701.0 jit_solution(7048355584428669658)
XLA Ops:
  7.2 0.7 convert_reduce_fusion
  8.0 1.2 copy.238
  9.6 0.7 copy.239
  10.8 0.7 copy.211
  11.6 0.7 fusion.168
  28.2 109.5 %all-gather.8.cloned.1.call-done = bf16[64,200,128]{2,1,0:T(8,128)(2,1)} async-done(((bf16[1,200,128]{2,1,0:T(8,128)(2,1)}), bf16[64,200,128]{2,1,0:T(8,128)(2,1)}) %all-gather.8.cloned.1.call-update) | async-done | bytes 3276816 | tf_op jit(solution)/shard_map/all_gather | solution.py:65
  137.7 1.0 constant_dynamic-slice_fusion.2
  141.1 121.1 %all-gather.4.cloned.1.call-done = bf16[64,200,128]{2,1,0:T(8,128)(2,1)} async-done(((bf16[1,200,128]{2,1,0:T(8,128)(2,1)}), bf16[64,200,128]{2,1,0:T(8,128)(2,1)}) %all-gather.4.cloned.1.call-update) | async-done | bytes 3276816 | tf_op jit(solution)/shard_map/all_gather | solution.py:65
  262.1 1.0 constant_dynamic-slice_fusion.18
  264.7 1.3 pad_maximum_fusion.7
  266.0 0.5 pad_maximum_fusion
  266.5 1.5 fusion.163
  268.5 0.5 maximum_maximum_fusion.2
  271.5 0.5 convolution_add_fusion.4
  273.0 1.2 fusion
  274.2 1.5 copy.252
  275.9 1.2 copy.253
  277.5 0.8 copy-done.29
  282.4 1.6 fusion.34
  284.0 1.3 copy.224
  285.4 0.7 copy.225
  286.4 2.0 fusion.23
  288.4 2.1 fusion.22
  290.4 1.0 fusion.21
  291.4 1.0 fusion.20
  292.4 1.0 fusion.19
  293.4 1.0 fusion.18
  294.3 1.0 fusion.17
  295.3 1.0 fusion.16
  296.3 1.0 fusion.15
  297.2 109.5 %all-gather.6.cloned.1.call-done = bf16[64,200,128]{2,1,0:T(8,128)(2,1)} async-done(((bf16[1,200,128]{2,1,0:T(8,128)(2,1)}), bf16[64,200,128]{2,1,0:T(8,128)(2,1)}) %all-gather.6.cloned.1.call-update) | async-done | bytes 3276816 | tf_op jit(solution)/shard_map/all_gather | solution.py:65
  406.7 1.0 constant_dynamic-slice_fusion.10
  409.3 0.5 pad_maximum_fusion.5
  409.8 0.5 pad_maximum_fusion.1
  411.3 1.2 fusion.14
  413.3 1.2 fusion.13
  414.8 1.2 fusion.12
  416.0 1.2 fusion.11
  417.2 1.2 fusion.10
  418.4 1.2 fusion.9
  419.6 1.2 fusion.8
  420.8 1.2 fusion.7
  422.0 1.2 fusion.6
  423.2 1.4 convolution_add_fusion.13
  426.8 1.1 fusion.5
  427.9 262.3 %all-reduce.3.cloned.1.call-done = (f32[9,200,200]{2,1,0:T(8,128)}, f32[9,200,200]{2,1,0:T(8,128)}) async-done(((f32[9,200,200]{2,1,0:T(8,128)}, f32[9,200,200]{2,1,0:T(8,128)}), (f32[9,200,200]{2,1,0:T(8,128)}, f32[9,200,200]{2,1,0:T(8,128)})) %all-reduce.3.cloned.1.call-update) | async-done | bytes 2880016 | tf_op jit(solution)/shard_map/psum | solution.py:166
  690.2 3.0 copy.333
  693.2 1.2 copy.334
  (209 shorter events, 19.0 us)
Async XLA Ops:
  7.2 3.2 copy-start.13
  7.2 130.6 %all-gather.8.cloned.1.call-start = ((), (), s32[]{:S(2)}) async-start(), calls=%async_computation.2 | async-start | bytes 3328000 | tf_op jit(solution)/shard_map/all_gather | solution.py:65
  9.2 129.5 %copy-start.2 = (bf16[1,1,200,1024]{2,3,1,0:T(8,128)(2,1)}, bf16[1,1,200,1024]{2,3,1,0:T(8,128)(2,1)S(1)}, u32[]{:S(2)}) copy-start(bf16[1,1,200,1024]{2,3,1,0:T(8,128)(2,1)S(1)} %copy.238) | copy-start | bytes 1228804
  9.3 2.3 copy-start.31
  9.3 2.3 copy-start.30
  10.4 251.8 %all-gather.4.cloned.1.call-start = ((), (), s32[]{:S(2)}) async-start(), calls=%async_computation | async-start | bytes 3328000 | tf_op jit(solution)/shard_map/all_gather | solution.py:65
  10.6 129.7 %copy-start = (bf16[9,200,200]{2,1,0:T(8,128)(2,1)S(1)}, bf16[9,200,200]{2,1,0:T(8,128)(2,1)}, u32[]{:S(2)}) copy-start(bf16[9,200,200]{2,1,0:T(8,128)(2,1)} %param.17) | copy-start | bytes 2160004
  11.5 395.2 %all-gather.6.cloned.1.call-start = ((), (), s32[]{:S(2)}) async-start(), calls=%async_computation.1 | async-start | bytes 3328000 | tf_op jit(solution)/shard_map/all_gather | solution.py:65
  270.4 1.0 copy-start.3
  277.1 1.2 copy-start.29
  277.5 1.1 copy-start.12
  277.5 1.5 copy-start.11
  277.5 1.5 copy-start.9
  278.6 1.0 copy-start.1
  279.0 1.0 copy-start.14
  280.0 1.0 copy-start.7
  280.3 1.1 copy-start.5
  281.1 1.1 copy-start.23
  281.1 1.3 copy-start.28
  284.0 6.4 copy-start.10
  286.2 404.1 %all-reduce.3.cloned.1.call-start = ((), (), s32[]{:S(2)}) async-start(), calls=%async_computation.3 | async-start | bytes 7372800 | tf_op jit(solution)/shard_map/psum | solution.py:166
  288.4 4.0 copy-start.15
  291.4 2.9 copy-start.8
  292.4 2.9 copy-start.6
  293.4 2.9 copy-start.24
  409.8 6.2 copy-start.16
  410.3 1.0 copy-start.4
  412.9 6.7 copy-start.21
  412.9 7.9 %copy-start.19 = (bf16[1,200,32,32]{1,3,2,0:T(8,128)(2,1)}, bf16[1,200,32,32]{1,3,2,0:T(8,128)(2,1)S(1)}, u32[]{:S(2)}) copy-start(bf16[1,200,32,32]{1,3,2,0:T(8,128)(2,1)S(1)} %get-tuple-element.62) | copy-start | bytes 1228804
  412.9 9.1 %copy-start.17 = (bf16[1,200,32,32]{1,3,2,0:T(8,128)(2,1)}, bf16[1,200,32,32]{1,3,2,0:T(8,128)(2,1)S(1)}, u32[]{:S(2)}) copy-start(bf16[1,200,32,32]{1,3,2,0:T(8,128)(2,1)S(1)} %get-tuple-element.61) | copy-start | bytes 1228804
  414.8 2.4 copy-start.26
  423.2 1.4 copy-start.27
  424.7 1.0 copy-start.22
  425.0 1.1 copy-start.20
  425.7 1.1 copy-start.18
  690.2 3.0 copy-start.25
Sparse Core Ops, SparseCore 0:
  12.0 125.6 all-gather.7
  141.8 120.3 all-gather.3
  286.3 120.4 all-gather.5
  423.4 266.8 all-reduce.2
where the time goes:
time: 702 us; the launch traced here: 701 us
  waiting for transfers between devices  602 us (86%)
  matrix products  35.5 us (5%)
  between operations  30.7 us (4%)
  local copies, waits for them, and re-layouts  26.9 us (4%)
    all_gather x3, waiting for transfers between devices, collect_rims(): lax.all_gather(strips, 'space', axis=0, tiled=True)  340 us
    psum x1, waiting for transfers between devices, body(): lax.psum((earlier_kernel_slope, latter_kernel_slope), ('space', 'dp'))  262 us
    dot_general x18, matrix products, weight_grad(): jnp.einsum('toc,tic->oi', grads, window(padded, k // 3 - 1, k % 3 - 1), p...  21.6 us
  transfers between devices with their start and end apart: 4, of which 4 were waited for; matrix products, arithmetic and copies ran while one was open for 3% of the time, Pallas kernels for 0%

commit v1 on v0

--- a/solution.py
+++ b/solution.py
@@ -62,7 +62,13 @@
 
 
 def collect_rims(strips, neighbours, fold_flag):
-    found = strip_parts(lax.all_gather(strips, "space", axis=0, tiled=True), neighbours, fold_flag)
+    found = strip_parts(
+        jnp.concatenate(
+            lax.all_to_all(jnp.stack([strips] * lax.axis_size("space")), "space", 0, 0), axis=0
+        ),
+        neighbours,
+        fold_flag,
+    )
     return tuple((b for b in found))
 
 

time: 702 us -> 609 us (0.87)
  waiting for transfers between devices: 602 us -> 457 us
  starting transfers between devices: 0.35 us -> 28.7 us
  local copies, waits for them, and re-layouts: 26.9 us -> 45.7 us
    all_gather x3 -> x0, waiting for transfers between devices: 340 us -> none  [collect_rims(): lax.all_gather(strips, 'space', axis=0, tiled=True)]
    all_to_all x0 -> x3, waiting for transfers between devices: none -> 195 us  [collect_rims(): lax.all_to_all(jnp.stack([strips] * lax.axis_size('space')), 'space', 0, 0)]
    all_to_all x0 -> x3, starting transfers between devices: none -> 28.6 us  [collect_rims(): lax.all_to_all(jnp.stack([strips] * lax.axis_size('space')), 'space', 0, 0)]
    all_to_all x0 -> x3, local copies, waits for them, and re-layouts: none -> 16.1 us  [collect_rims(): lax.all_to_all(jnp.stack([strips] * lax.axis_size('space')), 'space', 0, 0)]
  transfers between devices with their start and end apart: 4 -> 4, of which waited for: 4 -> 4; matrix products, arithmetic and copies ran while one was open for 3% -> 4% of each run, Pallas kernels for 0% -> 0%
where the time goes in v1:
time: 609 us; the launch traced here: 607 us
  waiting for transfers between devices  457 us (75%)
  local copies, waits for them, and re-layouts  45.7 us (8%)
  matrix products  35.9 us (6%)
  between operations  30.7 us (5%)
  starting transfers between devices  28.7 us (5%)
  other arithmetic  9.15 us (2%)
    psum x1, waiting for transfers between devices, body(): lax.psum((earlier_kernel_slope, latter_kernel_slope), ('space', 'dp'))  262 us
    all_to_all x3, waiting for transfers between devices, collect_rims(): lax.all_to_all(jnp.stack([strips] * lax.axis_size('space')), 'space', 0, 0)  195 us
    all_to_all x3, starting transfers between devices, collect_rims(): lax.all_to_all(jnp.stack([strips] * lax.axis_size('space')), 'space', 0, 0)  28.6 us
    dot_general x18, matrix products, weight_grad(): jnp.einsum('toc,tic->oi', grads, window(padded, k // 3 - 1, k % 3 - 1), p...  21.7 us
    all_to_all x3, local copies, waits for them, and re-layouts, collect_rims(): lax.all_to_all(jnp.stack([strips] * lax.axis_size('space')), 'space', 0, 0)  16.1 us
    unnamed x70, local copies, waits for them, and re-layouts  12.3 us
  transfers between devices with their start and end apart: 4, of which 4 were waited for; matrix products, arithmetic and copies ran while one was open for 4% of the time, Pallas kernels for 0%

profile of v1, /device:TPU:2, one launch (start us, length us, event | category | flops | bytes accessed | tf_op | source)
XLA Modules:
  0.0 606.9 jit_solution(6803219766860741295)
XLA Ops:
  7.2 1.2 copy.84
  8.6 2.1 stack.46
  10.7 13.8 %all-to-all-start = ((bf16[64,1,200,128]{3,2,1,0:T(8,128)(2,1)}), bf16[64,1,200,128]{3,2,1,0:T(8,128)(2,1)S(1)}, u32[]{:S(2)}, u32[]{:S(2)}) async-start(bf16[64,1,200,128]{3,2,1,0:T(8,128)(2,1)} %stack.46), calls=%async_computation | async-start | bytes 6553600 | tf_op jit(solution)/shard_map/all_to_all | solution.py:67
  24.6 2.0 copy.98
  26.7 1.2 multiply_convert_fusion.1
  28.8 72.9 %all-to-all-done = bf16[64,1,200,128]{3,2,1,0:T(8,128)(2,1)S(1)} async-done(((bf16[64,1,200,128]{3,2,1,0:T(8,128)(2,1)}), bf16[64,1,200,128]{3,2,1,0:T(8,128)(2,1)S(1)}, u32[]{:S(2)}, u32[]{:S(2)}) %all-to-all-start) | async-done | bytes 3276832 | tf_op jit(solution)/shard_map/all_to_all | solution.py:67
  101.7 2.1 stack.48
  103.9 7.5 %all-to-all-start.2 = ((bf16[64,1,200,128]{3,2,1,0:T(8,128)(2,1)}), bf16[64,1,200,128]{3,2,1,0:T(8,128)(2,1)}, u32[]{:S(2)}, u32[]{:S(2)}) async-start(bf16[64,1,200,128]{3,2,1,0:T(8,128)(2,1)} %stack.48), calls=%async_computation.2 | async-start | bytes 6553600 | tf_op jit(solution)/shard_map/all_to_all | solution.py:67
  128.1 4.2 copy.86
  132.3 55.9 %all-to-all-done.2 = bf16[64,1,200,128]{3,2,1,0:T(8,128)(2,1)} async-done(((bf16[64,1,200,128]{3,2,1,0:T(8,128)(2,1)}), bf16[64,1,200,128]{3,2,1,0:T(8,128)(2,1)}, u32[]{:S(2)}, u32[]{:S(2)}) %all-to-all-start.2) | async-done | bytes 3276832 | tf_op jit(solution)/shard_map/all_to_all | solution.py:67
  188.2 6.0 copy.100
  194.2 0.9 select_multiply_fusion
  195.3 0.8 fusion.121
  198.9 1.5 fusion.172
  205.4 1.2 fusion
  206.6 2.5 copy.105
  209.0 1.5 fusion.27
  210.6 2.4 copy.106
  213.4 0.8 copy-done.27
  218.3 1.6 fusion.34
  219.9 1.2 copy.91
  221.3 2.1 stack.47
  223.4 7.3 %all-to-all-start.1 = ((bf16[64,1,200,128]{3,2,1,0:T(8,128)(2,1)}), bf16[64,1,200,128]{3,2,1,0:T(8,128)(2,1)}, u32[]{:S(2)}, u32[]{:S(2)}) async-start(bf16[64,1,200,128]{3,2,1,0:T(8,128)(2,1)} %stack.47), calls=%async_computation.1 | async-start | bytes 6553600 | tf_op jit(solution)/shard_map/all_to_all | solution.py:67
  230.8 2.1 fusion.23
  232.8 2.1 fusion.22
  234.9 1.0 fusion.21
  235.9 1.0 fusion.20
  236.8 1.0 fusion.19
  237.8 1.0 fusion.18
  238.8 1.0 fusion.17
  239.8 1.0 fusion.16
  240.7 1.0 fusion.15
  241.7 65.8 %all-to-all-done.1 = bf16[64,1,200,128]{3,2,1,0:T(8,128)(2,1)} async-done(((bf16[64,1,200,128]{3,2,1,0:T(8,128)(2,1)}), bf16[64,1,200,128]{3,2,1,0:T(8,128)(2,1)}, u32[]{:S(2)}, u32[]{:S(2)}) %all-to-all-start.1) | async-done | bytes 3276832 | tf_op jit(solution)/shard_map/all_to_all | solution.py:67
  307.5 5.9 copy.93
  315.0 0.9 select_multiply_fusion.1
  318.0 1.2 fusion.14
  320.0 1.2 fusion.13
  321.5 1.2 fusion.12
  322.7 1.2 fusion.11
  323.9 1.2 fusion.10
  325.1 1.2 fusion.9
  326.3 1.2 fusion.8
  327.5 1.2 fusion.7
  328.7 1.2 fusion.6
  332.7 1.1 fusion.5
  333.7 262.0 %all-reduce.3.cloned.1.call-done = (f32[9,200,200]{2,1,0:T(8,128)}, f32[9,200,200]{2,1,0:T(8,128)}) async-done(((f32[9,200,200]{2,1,0:T(8,128)}, f32[9,200,200]{2,1,0:T(8,128)}), (f32[9,200,200]{2,1,0:T(8,128)}, f32[9,200,200]{2,1,0:T(8,128)})) %all-reduce.3.cloned.1.call-update) | async-done | bytes 2880016 | tf_op jit(solution)/shard_map/psum | solution.py:172
  595.8 3.0 copy.145
  598.8 1.2 copy.146
  (147 shorter events, 21.5 us)
Async XLA Ops:
  8.4 2.3 copy-start.1
  10.7 13.8 %copy-start.29 = (s32[1,1024]{1,0:T(1,128)S(1)}, s32[1,1024]{1,0:T(1,128)}, u32[]{:S(2)}) copy-start(s32[1,1024]{1,0:T(1,128)} %param.13) | copy-start | bytes 12292
  10.7 91.0 %all-to-all-start = ((bf16[64,1,200,128]{3,2,1,0:T(8,128)(2,1)}), bf16[64,1,200,128]{3,2,1,0:T(8,128)(2,1)S(1)}, u32[]{:S(2)}, u32[]{:S(2)}) async-start(bf16[64,1,200,128]{3,2,1,0:T(8,128)(2,1)} %stack.46), calls=%async_computation | async-start | bytes 6553600 | tf_op jit(solution)/shard_map/all_to_all | solution.py:67
  27.9 0.8 copy-start.3
  103.9 7.6 %copy-start.28 = (s32[1,8]{1,0:T(1,128)S(1)}, s32[1,8]{1,0:T(1,128)}, u32[]{:S(2)}) copy-start(s32[1,8]{1,0:T(1,128)} %param.14) | copy-start | bytes 100
  103.9 84.3 %all-to-all-start.2 = ((bf16[64,1,200,128]{3,2,1,0:T(8,128)(2,1)}), bf16[64,1,200,128]{3,2,1,0:T(8,128)(2,1)}, u32[]{:S(2)}, u32[]{:S(2)}) async-start(bf16[64,1,200,128]{3,2,1,0:T(8,128)(2,1)} %stack.48), calls=%async_computation.2 | async-start | bytes 6553600 | tf_op jit(solution)/shard_map/all_to_all | solution.py:67
  132.3 64.9 %copy-start = (bf16[9,200,200]{2,1,0:T(8,128)(2,1)S(1)}, bf16[9,200,200]{2,1,0:T(8,128)(2,1)}, u32[]{:S(2)}) copy-start(bf16[9,200,200]{2,1,0:T(8,128)(2,1)} %param.17) | copy-start | bytes 2160004
  194.2 3.7 copy-start.2
  198.9 1.6 copy-start.4
  202.8 1.0 copy-start.5
  213.0 1.2 copy-start.27
  213.4 1.5 copy-start.13
  213.4 1.5 copy-start.14
  213.4 1.5 copy-start.11
  214.9 1.0 copy-start.15
  215.9 1.0 copy-start.9
  216.2 1.1 copy-start.7
  216.9 1.1 copy-start.21
  216.9 1.3 copy-start.26
  223.4 84.1 %all-to-all-start.1 = ((bf16[64,1,200,128]{3,2,1,0:T(8,128)(2,1)}), bf16[64,1,200,128]{3,2,1,0:T(8,128)(2,1)}, u32[]{:S(2)}, u32[]{:S(2)}) async-start(bf16[64,1,200,128]{3,2,1,0:T(8,128)(2,1)} %stack.47), calls=%async_computation.1 | async-start | bytes 6553600 | tf_op jit(solution)/shard_map/all_to_all | solution.py:67
  230.7 365.1 %all-reduce.3.cloned.1.call-start = ((), (), s32[]{:S(2)}) async-start(), calls=%async_computation.3 | async-start | bytes 7372800 | tf_op jit(solution)/shard_map/psum | solution.py:172
  230.8 4.1 copy-start.12
  232.8 4.0 copy-start.16
  235.9 2.9 copy-start.10
  236.8 2.9 copy-start.8
  237.8 2.9 copy-start.22
  317.0 1.0 copy-start.6
  319.6 6.7 %copy-start.19 = (bf16[1,200,32,32]{1,3,2,0:T(8,128)(2,1)}, bf16[1,200,32,32]{1,3,2,0:T(8,128)(2,1)S(1)}, u32[]{:S(2)}) copy-start(bf16[1,200,32,32]{1,3,2,0:T(8,128)(2,1)S(1)} %get-tuple-element.60) | copy-start | bytes 1228804
  319.6 7.9 %copy-start.17 = (bf16[1,200,32,32]{1,3,2,0:T(8,128)(2,1)}, bf16[1,200,32,32]{1,3,2,0:T(8,128)(2,1)S(1)}, u32[]{:S(2)}) copy-start(bf16[1,200,32,32]{1,3,2,0:T(8,128)(2,1)S(1)} %get-tuple-element.59) | copy-start | bytes 1228804
  321.5 2.4 copy-start.24
  329.9 1.0 copy-start.25
  330.9 1.0 copy-start.20
  331.2 1.1 copy-start.18
  595.8 3.0 copy-start.23
Sparse Core Ops, SparseCore 0:
  330.0 265.7 all-reduce.2
